TPU v7x, 128 devices: a whole 4x4x4 slice. The times are simulated.
128 devices in a mesh: dp: 16 (over x_lo, z, core), tensor: 8 (over y, x_hi).
Axes of the slice: x: 4 (x_hi: 2, x_lo: 2; x = x_hi * 2 + x_lo), y: 4, z: 4, core: 2. Of those that a mesh axis runs over, the one named last changes fastest.
Arguments:
- tokens: bfloat16 [12288, 1024], P('dp'), may hold values from -72 to 72
- w_qkv: float32 [1024, 3072], P(('dp', 'tensor')), may hold values from -0.1875 to 0.1875
- w_out: float32 [1024, 1024], P(None, ('dp', 'tensor')), may hold values from -0.1875 to 0.1875
- w_up: float32 [1024, 4096], P(('dp', 'tensor')), may hold values from -0.1875 to 0.1875
- w_down: float32 [4096, 1024], P(None, ('dp', 'tensor')), may hold values from -0.09375 to 0.09375
- slot_request: int32 [96, 128], replicated, may hold values from -1 to 3, as said below
Outputs:
- encoded: bfloat16 [12288, 1024], P('dp')
Inputs may be any that keep to these rules, and one draw needn't show every extreme that they name: `slot_request`: requests are numbered 0 to 3, all present; each request holds 1 to 48 pages and one holds exactly 48; each request's pages are full except its last page, whose empty slots are its final ones; pages may sit in any slot of the table.
All inputs are finite; a program needn't handle non-finite values.
Results may differ from a plain program's by a relative error of at most 0.025.
The roundings to bfloat16 on the way count: a program that leaves them out, or rounds other values in their place, can miss the bound.
Values may be sent and summed in bfloat16 or wider, within the bound.
No kernel may reach another device: no remote copies, remote signals or barrier semaphores. Data moves between devices by JAX's collectives and lax.ppermute only.
A program may use at most 128 MiB of HBM per device.

v0:
```python
import math
import jax
import jax.numpy as jnp
from jax import lax
from jax.sharding import PartitionSpec as P

D = 1024
H = 16


def layer_norm(value):
    mean = jnp.mean(value, axis=-1, keepdims=True)
    centred = value - mean
    spread = jnp.mean(centred * centred, axis=-1, keepdims=True)
    return centred * lax.rsqrt(spread + 1e-05)


def shards(tokens, w_qkv, w_out, w_up, w_down, slot_request):
    groups = lax.axis_size("tensor")
    tensor_rank = lax.axis_index("tensor")
    row_split = (w_qkv.astype(jnp.bfloat16), w_up.astype(jnp.bfloat16))
    col_split = (w_out.astype(jnp.bfloat16), w_down.astype(jnp.bfloat16))
    qkv_full, up_full = (
        lax.all_gather(row_split[0], ("dp", "tensor"), axis=0, tiled=True),
        lax.all_gather(row_split[1], ("dp", "tensor"), axis=0, tiled=True),
    )
    out_full, down_full = (
        lax.all_gather(col_split[0], ("dp", "tensor"), axis=1, tiled=True),
        lax.all_gather(col_split[1], ("dp", "tensor"), axis=1, tiled=True),
    )
    qkv_cols = qkv_full.shape[1] // groups
    up_cols = up_full.shape[1] // groups
    out_rows = out_full.shape[0] // groups
    down_rows = down_full.shape[0] // groups
    qkv_block = lax.dynamic_slice_in_dim(qkv_full, tensor_rank * qkv_cols, qkv_cols, 1)
    up_block = lax.dynamic_slice_in_dim(up_full, tensor_rank * up_cols, up_cols, 1)
    out_block = lax.dynamic_slice_in_dim(out_full, tensor_rank * out_rows, out_rows, 0)
    down_block = lax.dynamic_slice_in_dim(down_full, tensor_rank * down_rows, down_rows, 0)
    tok_rows = tokens.shape[0]
    head_size = D // H
    heads_here = qkv_block.shape[1] // (3 * head_size)
    qkv = jnp.dot(tokens, qkv_block, preferred_element_type=jnp.float32).astype(jnp.bfloat16)
    qkv = qkv.reshape(tok_rows, heads_here, 3, head_size)
    queries = qkv[:, :, 0, :]
    key_rows = qkv[:, :, 1, :].reshape(tok_rows, heads_here * head_size)
    value_rows = qkv[:, :, 2, :].reshape(tok_rows, heads_here * head_size)
    slot_ids = slot_request.reshape(-1)
    own_ids = lax.dynamic_slice_in_dim(slot_ids, lax.axis_index("dp") * tok_rows, tok_rows, 0)
    scale = 1.0 / math.sqrt(head_size)

    def update(carry, key_block, value_block, key_ids):
        running_max, total, accumulated = carry
        width = key_block.shape[0]
        key_heads = key_block.reshape(width, heads_here, head_size)
        value_heads = value_block.reshape(width, heads_here, head_size)
        scores = (
            jnp.einsum("qhd,khd->hqk", queries, key_heads, preferred_element_type=jnp.float32)
            * scale
        )
        allowed = (own_ids[:, None] == key_ids[None, :])[None]
        masked = jnp.where(allowed, scores, -1e30)
        new_max = jnp.maximum(running_max, jnp.max(masked, axis=-1))
        weights = jnp.where(allowed, jnp.exp(masked - new_max[..., None]), 0.0)
        rescale = jnp.exp(running_max - new_max)
        total = total * rescale + jnp.sum(weights, axis=-1)
        mixed = jnp.einsum(
            "hqk,khd->qhd",
            weights.astype(jnp.bfloat16),
            value_heads,
            preferred_element_type=jnp.float32,
        )
        accumulated = accumulated * jnp.transpose(rescale)[..., None] + mixed
        return (new_max, total, accumulated)

    def visit(carry, key_block, value_block, key_ids):
        return update(carry, key_block, value_block, key_ids)

    initial = (
        jnp.full((heads_here, tok_rows), -1e30, jnp.float32),
        jnp.zeros((heads_here, tok_rows), jnp.float32),
        jnp.zeros((tok_rows, heads_here, head_size), jnp.float32),
    )
    key_piece = lax.all_gather(key_rows, "dp", axis=0, tiled=True)
    value_piece = lax.all_gather(value_rows, "dp", axis=0, tiled=True)
    key_count = key_piece.shape[0]
    steps = key_count // tok_rows
    piece_ids = slot_ids.reshape(steps, tok_rows)
    key_steps = key_piece.reshape(steps, tok_rows, key_piece.shape[1])
    value_steps = value_piece.reshape(steps, tok_rows, value_piece.shape[1])

    def one_step(state, inputs):
        key_block, value_block, key_ids = inputs
        return (visit(state, key_block, value_block, key_ids), None)

    result, unused = lax.scan(one_step, initial, (key_steps, value_steps, piece_ids))
    running_max, total, accumulated = result
    attn = (
        (accumulated / jnp.transpose(total)[..., None])
        .astype(jnp.bfloat16)
        .reshape(tok_rows, heads_here * head_size)
    )
    proj = lax.psum(
        jnp.dot(attn, out_block, preferred_element_type=jnp.float32).astype(jnp.bfloat16), "tensor"
    ).astype(jnp.float32)
    first = layer_norm(tokens.astype(jnp.float32) + proj).astype(jnp.bfloat16)
    inner = jax.nn.gelu(
        jnp.dot(first, up_block, preferred_element_type=jnp.float32), approximate=False
    ).astype(jnp.bfloat16)
    ffn = lax.psum(
        jnp.dot(inner, down_block, preferred_element_type=jnp.float32).astype(jnp.bfloat16),
        "tensor",
    ).astype(jnp.float32)
    live = (own_ids >= 0).astype(jnp.float32)[:, None]
    encoded = (layer_norm(first.astype(jnp.float32) + ffn) * live).astype(jnp.bfloat16)
    return encoded


def solution(mesh):
    in_specs = (
        P("dp", None),
        P(("dp", "tensor"), None),
        P(None, ("dp", "tensor")),
        P(("dp", "tensor"), None),
        P(None, ("dp", "tensor")),
        P(),
    )
    out_specs = P("dp", None)
    return jax.shard_map(shards, mesh=mesh, in_specs=in_specs, out_specs=out_specs, check_vma=False)
```

profile of v0, /device:TPU:0, one launch (start us, length us, event | category | flops | bytes accessed | tf_op | source)
XLA Modules:
  0.0 1536.8 jit_solution(17673529418651723079)
XLA Ops:
  8.1 309.5 %all-gather.7.cloned.1.call-done = bf16[1024,3072]{1,0:T(8,128)(2,1)} async-done(((bf16[8,3072]{1,0:T(8,128)(2,1)}), bf16[1024,3072]{1,0:T(8,128)(2,1)}) %all-gather.7.cloned.1.call-update) | async-done | bytes 6291472 | tf_op jit(solution)/shard_map/all_gather | solution.py:24
  322.6 35.3 %all-gather.9.cloned.1.call-done = bf16[12288,128]{0,1:T(8,128)(2,1)} async-done(((bf16[768,128]{0,1:T(8,128)(2,1)}), bf16[12288,128]{0,1:T(8,128)(2,1)}) %all-gather.9.cloned.1.call-update) | async-done | bytes 3145744 | tf_op jit(solution)/shard_map/all_gather | solution.py:83
  357.8 4.7 copy.17
  362.5 32.4 %all-gather.11.cloned.1.call-done = bf16[12288,128]{0,1:T(8,128)(2,1)} async-done(((bf16[768,128]{0,1:T(8,128)(2,1)}), bf16[12288,128]{0,1:T(8,128)(2,1)}) %all-gather.11.cloned.1.call-update) | async-done | bytes 3145744 | tf_op jit(solution)/shard_map/all_gather | solution.py:84
  394.9 4.7 copy.20
  399.6 165.9 %while.15 = (s32[]{:T(128)}, f32[2,768]{1,0:T(2,128)S(1)}, f32[2,768]{1,0:T(2,128)S(1)}, f32[768,2,64]{0,2,1:T(8,128)S(1)}, s32[768]{0:T(1024)S(1)}, /*index=5*/...) while((s32[]{:T(128)}, f32[2,768]{1,0:T(2,128)S(1)}, ...), condition=%wide.region_3.4_spmd.clone, body=%wide.region_0.3_spmd.clone.sunk | while | flops 318219264 | bytes 33730736 | solution.py:95
  404.6 4.0 fusion.130
  415.0 4.0 fusion.130
  425.4 4.0 fusion.130
  432.4 3.2 fusion.126
  435.7 4.0 fusion.130
  442.7 3.2 fusion.126
  446.1 4.0 fusion.130
  456.5 4.0 fusion.130
  466.8 4.0 fusion.130
  477.2 4.0 fusion.130
  484.2 3.2 fusion.126
  487.6 4.0 fusion.130
  494.6 3.2 fusion.126
  497.9 4.0 fusion.130
  508.3 4.0 fusion.130
  518.7 4.0 fusion.130
  529.0 4.0 fusion.130
  539.4 4.0 fusion.130
  549.8 4.0 fusion.130
  560.2 4.0 fusion.130
  565.5 132.8 %all-gather.13.cloned.1.call-done = bf16[1024,1024]{0,1:T(8,128)(2,1)} async-done(((bf16[1024,8]{0,1:T(8,128)(2,1)}), bf16[1024,1024]{0,1:T(8,128)(2,1)}) %all-gather.13.cloned.1.call-update) | async-done | bytes 2097168 | tf_op jit(solution)/shard_map/all_gather | solution.py:28
  702.9 96.7 %all-reduce.3.cloned.1.call-done = bf16[768,1024]{1,0:T(8,128)(2,1)} async-done(((bf16[768,1024]{1,0:T(8,128)(2,1)}), bf16[768,1024]{1,0:T(8,128)(2,1)}) %all-reduce.3.cloned.1.call-update) | async-done | bytes 1572880 | tf_op jit(solution)/shard_map/psum | solution.py:102
  803.0 305.4 %all-gather.15.cloned.1.call-done = bf16[1024,4096]{1,0:T(8,128)(2,1)} async-done(((bf16[8,4096]{1,0:T(8,128)(2,1)}), bf16[1024,4096]{1,0:T(8,128)(2,1)}) %all-gather.15.cloned.1.call-update) | async-done | bytes 8388624 | tf_op jit(solution)/shard_map/all_gather | solution.py:25
  1108.4 311.5 %all-gather.17.cloned.1.call-done = bf16[4096,1024]{0,1:T(8,128)(2,1)} async-done(((bf16[4096,8]{0,1:T(8,128)(2,1)}), bf16[4096,1024]{0,1:T(8,128)(2,1)}) %all-gather.17.cloned.1.call-update) | async-done | bytes 8388624 | tf_op jit(solution)/shard_map/all_gather | solution.py:29
  1419.9 7.6 convolution_convert_fusion
  1427.6 97.8 %all-reduce.5.cloned.1.call-done = bf16[768,1024]{1,0:T(8,128)(2,1)} async-done(((bf16[768,1024]{1,0:T(8,128)(2,1)}), bf16[768,1024]{1,0:T(8,128)(2,1)}) %all-reduce.5.cloned.1.call-update) | async-done | bytes 1572880 | tf_op jit(solution)/shard_map/psum | solution.py:109
  (289 shorter events, 105.9 us)
Async XLA Ops:
  6.5 311.1 %all-gather.7.cloned.1.call-start = ((), (), s32[]{:S(2)}) async-start(), calls=%async_computation | async-start | bytes 6340608 | tf_op jit(solution)/shard_map/all_gather | solution.py:24
  8.1 349.8 %all-gather.9.cloned.1.call-start = ((), (), s32[]{:S(2)}) async-start(), calls=%async_computation.1 | async-start | bytes 3342336 | tf_op jit(solution)/shard_map/all_gather | solution.py:83
  321.0 74.0 %all-gather.11.cloned.1.call-start = ((), (), s32[]{:S(2)}) async-start(), calls=%async_computation.2 | async-start | bytes 3342336 | tf_op jit(solution)/shard_map/all_gather | solution.py:84
  321.7 376.7 %all-gather.13.cloned.1.call-start = ((), (), s32[]{:S(2)}) async-start(), calls=%async_computation.3 | async-start | bytes 2113536 | tf_op jit(solution)/shard_map/all_gather | solution.py:28
  322.4 477.2 %all-reduce.3.cloned.1.call-start = ((), (), s32[]{:S(2)}) async-start(), calls=%async_computation.4 | async-start | bytes 3145728 | tf_op jit(solution)/shard_map/psum | solution.py:102
  404.5 4.2 slice-start
  404.6 4.1 slice-start.1
  414.8 4.2 slice-start
  425.2 4.2 slice-start
  435.6 4.2 slice-start
  445.9 4.2 slice-start
  456.3 4.2 slice-start
  466.7 4.2 slice-start
  477.0 4.2 slice-start
  487.4 4.2 slice-start
  487.6 4.1 slice-start.1
  497.8 4.2 slice-start
  497.9 4.1 slice-start.1
  508.1 4.2 slice-start
  518.5 4.2 slice-start
  528.9 4.2 slice-start
  529.0 4.1 slice-start.1
  539.2 4.2 slice-start
  539.4 4.1 slice-start.1
  549.6 4.2 slice-start
  549.8 4.1 slice-start.1
  560.0 4.2 slice-start
  560.1 4.1 slice-start.1
  698.4 101.2 %copy-start = (bf16[768,1024]{1,0:T(8,128)(2,1)S(1)}, bf16[768,1024]{1,0:T(8,128)(2,1)}, u32[]{:S(2)}) copy-start(bf16[768,1024]{1,0:T(8,128)(2,1)} %param.8) | copy-start | bytes 4718596
  701.2 407.2 %all-gather.15.cloned.1.call-start = ((), (), s32[]{:S(2)}) async-start(), calls=%async_computation.5 | async-start | bytes 8454144 | tf_op jit(solution)/shard_map/all_gather | solution.py:25
  701.9 718.0 %all-gather.17.cloned.1.call-start = ((), (), s32[]{:S(2)}) async-start(), calls=%async_computation.6 | async-start | bytes 8454144 | tf_op jit(solution)/shard_map/all_gather | solution.py:29
  702.7 822.7 %all-reduce.5.cloned.1.call-start = ((), (), s32[]{:S(2)}) async-start(), calls=%async_computation.7 | async-start | bytes 3145728 | tf_op jit(solution)/shard_map/psum | solution.py:109
  (15 other events, 51.0 us)
Sparse Core Ops, SparseCore 0:
  9.0 308.5 all-gather.6
  321.1 36.7 all-gather.8
  359.5 35.3 all-gather.10
  396.5 301.8 all-gather.12
  701.3 98.2 all-reduce.2
  801.1 307.2 all-gather.14
  1110.1 309.7 all-gather.16
  1427.7 97.5 all-reduce.4
where the time goes:
time: 1540 us
  waiting for transfers between devices  1320 us (86%)
  matrix products  128 us (8%)
  other arithmetic  38.2 us (2%)
  local copies, waits for them, and re-layouts  32.3 us (2%)
    all_gather x1, waiting for transfers between devices, shards(): lax.all_gather(col_split[1], ('dp', 'tensor'), axis=1, tiled=True)  312 us
    all_gather x1, waiting for transfers between devices, shards(): lax.all_gather(row_split[0], ('dp', 'tensor'), axis=0, tiled=True)  309 us
    all_gather x1, waiting for transfers between devices, shards(): lax.all_gather(row_split[1], ('dp', 'tensor'), axis=0, tiled=True)  305 us
    all_gather x1, waiting for transfers between devices, shards(): lax.all_gather(col_split[0], ('dp', 'tensor'), axis=1, tiled=True)  133 us
    psum x1, waiting for transfers between devices, shards(): lax.psum(jnp.dot(inner, down_block, preferred_element_type=jnp.float32).a...  97.8 us
    psum x1, waiting for transfers between devices, shards(): lax.psum(jnp.dot(attn, out_block, preferred_element_type=jnp.float32).ast...  96.7 us
    dot_general x16, matrix products, update(): jnp.einsum('hqk,khd->qhd', weights.astype(jnp.bfloat16), value_heads, pre...  64.5 us
    dot_general x16, matrix products, update(): jnp.einsum('qhd,khd->hqk', queries, key_heads, preferred_element_type=jnp...  50.9 us
  transfers between devices with their start and end apart: 8, of which 8 were waited for; matrix products, arithmetic and copies ran while one was open for 12% of the time, Pallas kernels for 0%

commit v1 on v0

--- a/solution.py
+++ b/solution.py
@@ -106,9 +106,12 @@
     inner = jax.nn.gelu(
         jnp.dot(first, up_block, preferred_element_type=jnp.float32), approximate=False
     ).astype(jnp.bfloat16)
-    ffn = lax.psum(
-        jnp.dot(inner, down_block, preferred_element_type=jnp.float32).astype(jnp.bfloat16),
-        "tensor",
+    ffn = jnp.sum(
+        lax.all_gather(
+            jnp.dot(inner, down_block, preferred_element_type=jnp.float32).astype(jnp.bfloat16),
+            "tensor",
+        ),
+        axis=0,
     ).astype(jnp.float32)
     live = (own_ids >= 0).astype(jnp.float32)[:, None]
     encoded = (layer_norm(first.astype(jnp.float32) + ffn) * live).astype(jnp.bfloat16)

time: 1540 us -> 1590 us (1.032)
  waiting for transfers between devices: 1320 us -> 1370 us
    all_gather x0 -> x1, waiting for transfers between devices: none -> 146 us  [shards(): lax.all_gather(jnp.dot(inner, down_block, preferred_element_type=jnp.floa...]
    psum x1 -> x0, waiting for transfers between devices: 97.8 us -> none  [shards(): lax.psum(jnp.dot(inner, down_block, preferred_element_type=jnp.float32).a...]
  transfers between devices with their start and end apart: 8 -> 8, of which waited for: 8 -> 8; matrix products, arithmetic and copies ran while one was open for 12% -> 11% of each run, Pallas kernels for 0% -> 0%
where the time goes in v1:
time: 1590 us
  waiting for transfers between devices  1370 us (86%)
  matrix products  128 us (8%)
  other arithmetic  45 us (3%)
  local copies, waits for them, and re-layouts  32.3 us (2%)
    all_gather x1, waiting for transfers between devices, shards(): lax.all_gather(col_split[1], ('dp', 'tensor'), axis=1, tiled=True)  312 us
    all_gather x1, waiting for transfers between devices, shards(): lax.all_gather(row_split[0], ('dp', 'tensor'), axis=0, tiled=True)  309 us
    all_gather x1, waiting for transfers between devices, shards(): lax.all_gather(row_split[1], ('dp', 'tensor'), axis=0, tiled=True)  305 us
    all_gather x1, waiting for transfers between devices, shards(): lax.all_gather(jnp.dot(inner, down_block, preferred_element_type=jnp.floa...  146 us
    all_gather x1, waiting for transfers between devices, shards(): lax.all_gather(col_split[0], ('dp', 'tensor'), axis=1, tiled=True)  132 us
    psum x1, waiting for transfers between devices, shards(): lax.psum(jnp.dot(attn, out_block, preferred_element_type=jnp.float32).ast...  96.3 us
    dot_general x16, matrix products, update(): jnp.einsum('hqk,khd->qhd', weights.astype(jnp.bfloat16), value_heads, pre...  64.5 us
    dot_general x16, matrix products, update(): jnp.einsum('qhd,khd->hqk', queries, key_heads, preferred_element_type=jnp...  50.9 us
  transfers between devices with their start and end apart: 8, of which 8 were waited for; matrix products, arithmetic and copies ran while one was open for 11% of the time, Pallas kernels for 0%

profile of v1, /device:TPU:0, one launch (start us, length us, event | category | flops | bytes accessed | tf_op | source)
XLA Modules:
  0.0 1590.7 jit_solution(2955156019106034959)
XLA Ops:
  8.1 309.5 %all-gather.9.cloned.1.call-done = bf16[1024,3072]{1,0:T(8,128)(2,1)} async-done(((bf16[8,3072]{1,0:T(8,128)(2,1)}), bf16[1024,3072]{1,0:T(8,128)(2,1)}) %all-gather.9.cloned.1.call-update) | async-done | bytes 6291472 | tf_op jit(solution)/shard_map/all_gather | solution.py:24
  322.6 35.3 %all-gather.11.cloned.1.call-done = bf16[12288,128]{0,1:T(8,128)(2,1)} async-done(((bf16[768,128]{0,1:T(8,128)(2,1)}), bf16[12288,128]{0,1:T(8,128)(2,1)}) %all-gather.11.cloned.1.call-update) | async-done | bytes 3145744 | tf_op jit(solution)/shard_map/all_gather | solution.py:83
  357.8 4.7 copy.17
  362.5 32.4 %all-gather.13.cloned.1.call-done = bf16[12288,128]{0,1:T(8,128)(2,1)} async-done(((bf16[768,128]{0,1:T(8,128)(2,1)}), bf16[12288,128]{0,1:T(8,128)(2,1)}) %all-gather.13.cloned.1.call-update) | async-done | bytes 3145744 | tf_op jit(solution)/shard_map/all_gather | solution.py:84
  394.9 4.7 copy.20
  399.7 165.9 %while.15 = (s32[]{:T(128)}, f32[2,768]{1,0:T(2,128)S(1)}, f32[2,768]{1,0:T(2,128)S(1)}, f32[768,2,64]{0,2,1:T(8,128)S(1)}, s32[768]{0:T(1024)S(1)}, /*index=5*/...) while((s32[]{:T(128)}, f32[2,768]{1,0:T(2,128)S(1)}, ...), condition=%wide.region_3.4_spmd.clone, body=%wide.region_0.3_spmd.clone.sunk | while | flops 318219264 | bytes 33730736 | solution.py:95
  404.7 4.0 fusion.130
  415.1 4.0 fusion.130
  422.0 3.2 fusion.126
  425.4 4.0 fusion.130
  435.8 4.0 fusion.130
  442.8 3.2 fusion.126
  446.2 4.0 fusion.130
  456.5 4.0 fusion.130
  466.9 4.0 fusion.130
  477.3 4.0 fusion.130
  487.6 4.0 fusion.130
  494.6 3.2 fusion.126
  498.0 4.0 fusion.130
  508.4 4.0 fusion.130
  518.8 4.0 fusion.130
  529.1 4.0 fusion.130
  539.5 4.0 fusion.130
  549.9 4.0 fusion.130
  560.3 4.0 fusion.130
  565.6 132.3 %all-gather.15.cloned.1.call-done = bf16[1024,1024]{0,1:T(8,128)(2,1)} async-done(((bf16[1024,8]{0,1:T(8,128)(2,1)}), bf16[1024,1024]{0,1:T(8,128)(2,1)}) %all-gather.15.cloned.1.call-update) | async-done | bytes 2097168 | tf_op jit(solution)/shard_map/all_gather | solution.py:28
  702.5 96.3 %all-reduce.2.cloned.1.call-done = bf16[768,1024]{1,0:T(8,128)(2,1)} async-done(((bf16[768,1024]{1,0:T(8,128)(2,1)}), bf16[768,1024]{1,0:T(8,128)(2,1)}) %all-reduce.2.cloned.1.call-update) | async-done | bytes 1572880 | tf_op jit(solution)/shard_map/psum | solution.py:102
  802.2 305.4 %all-gather.17.cloned.1.call-done = bf16[1024,4096]{1,0:T(8,128)(2,1)} async-done(((bf16[8,4096]{1,0:T(8,128)(2,1)}), bf16[1024,4096]{1,0:T(8,128)(2,1)}) %all-gather.17.cloned.1.call-update) | async-done | bytes 8388624 | tf_op jit(solution)/shard_map/all_gather | solution.py:25
  1107.6 311.5 %all-gather.19.cloned.1.call-done = bf16[4096,1024]{0,1:T(8,128)(2,1)} async-done(((bf16[4096,8]{0,1:T(8,128)(2,1)}), bf16[4096,1024]{0,1:T(8,128)(2,1)}) %all-gather.19.cloned.1.call-update) | async-done | bytes 8388624 | tf_op jit(solution)/shard_map/all_gather | solution.py:29
  1419.1 7.6 convolution_convert_fusion
  1426.8 145.6 %all-gather.21.cloned.1.call-done = bf16[6144,1024]{1,0:T(8,128)(2,1)} async-done(((bf16[768,1024]{1,0:T(8,128)(2,1)}), bf16[6144,1024]{1,0:T(8,128)(2,1)}) %all-gather.21.cloned.1.call-update) | async-done | bytes 12582928 | tf_op jit(solution)/shard_map/all_gather | solution.py:110
  1572.4 8.4 reduce_sum.59
  (288 shorter events, 107.5 us)
Async XLA Ops:
  6.5 311.1 %all-gather.9.cloned.1.call-start = ((), (), s32[]{:S(2)}) async-start(), calls=%async_computation | async-start | bytes 6340608 | tf_op jit(solution)/shard_map/all_gather | solution.py:24
  8.1 349.8 %all-gather.11.cloned.1.call-start = ((), (), s32[]{:S(2)}) async-start(), calls=%async_computation.1 | async-start | bytes 3342336 | tf_op jit(solution)/shard_map/all_gather | solution.py:83
  321.0 74.0 %all-gather.13.cloned.1.call-start = ((), (), s32[]{:S(2)}) async-start(), calls=%async_computation.2 | async-start | bytes 3342336 | tf_op jit(solution)/shard_map/all_gather | solution.py:84
  321.7 376.2 %all-gather.15.cloned.1.call-start = ((), (), s32[]{:S(2)}) async-start(), calls=%async_computation.3 | async-start | bytes 2113536 | tf_op jit(solution)/shard_map/all_gather | solution.py:28
  322.4 476.4 %all-reduce.2.cloned.1.call-start = ((), (), s32[]{:S(2)}) async-start(), calls=%async_computation.4 | async-start | bytes 3145728 | tf_op jit(solution)/shard_map/psum | solution.py:102
  404.5 4.2 slice-start
  404.7 4.1 slice-start.1
  414.9 4.2 slice-start
  425.3 4.2 slice-start
  435.6 4.2 slice-start
  446.0 4.2 slice-start
  456.4 4.2 slice-start
  466.7 4.2 slice-start
  477.1 4.2 slice-start
  477.2 4.1 slice-start.1
  487.5 4.2 slice-start
  487.6 4.1 slice-start.1
  497.8 4.2 slice-start
  498.0 4.1 slice-start.1
  508.2 4.2 slice-start
  508.4 4.1 slice-start.1
  518.6 4.2 slice-start
  529.0 4.2 slice-start
  539.3 4.2 slice-start
  539.5 4.1 slice-start.1
  549.7 4.2 slice-start
  549.9 4.1 slice-start.1
  560.1 4.2 slice-start
  697.9 100.9 %copy-start = (bf16[768,1024]{1,0:T(8,128)(2,1)S(1)}, bf16[768,1024]{1,0:T(8,128)(2,1)}, u32[]{:S(2)}) copy-start(bf16[768,1024]{1,0:T(8,128)(2,1)} %param.8) | copy-start | bytes 4718596
  700.8 406.8 %all-gather.17.cloned.1.call-start = ((), (), s32[]{:S(2)}) async-start(), calls=%async_computation.5 | async-start | bytes 8454144 | tf_op jit(solution)/shard_map/all_gather | solution.py:25
  701.5 717.6 %all-gather.19.cloned.1.call-start = ((), (), s32[]{:S(2)}) async-start(), calls=%async_computation.6 | async-start | bytes 8454144 | tf_op jit(solution)/shard_map/all_gather | solution.py:29
  702.3 870.1 %all-gather.21.cloned.1.call-start = ((), (), s32[]{:S(2)}) async-start(), calls=%async_computation.7 | async-start | bytes 14155776 | tf_op jit(solution)/shard_map/all_gather | solution.py:110
  (14 other events, 49.0 us)
Sparse Core Ops, SparseCore 0:
  9.0 308.5 all-gather.8
  321.1 36.7 all-gather.10
  359.5 35.3 all-gather.12
  396.5 301.4 all-gather.14
  700.9 97.8 all-reduce.1
  800.3 307.2 all-gather.16
  1109.3 309.7 all-gather.18
  1426.9 145.4 all-gather.20
